TPU v7x, 512 devices: a whole 4x8x8 slice. The times are simulated.
512 devices in a mesh: expert: 128 (over z, y, core), tensor: 4 (over x).
Axes of the slice: x: 4, y: 8, z: 8, core: 2. Of those that a mesh axis runs over, the one named last changes fastest.
Arguments:
- attn_partial: bfloat16 [4, 4096, 3584], P('tensor', 'expert'), may hold values from -4 to 4
- residual_in: bfloat16 [4096, 3584], P(('expert', 'tensor')), may hold values from -6 to 6
- norm_gain: bfloat16 [3584], replicated, may hold values from 0.25 to 1.75
- w_in: bfloat16 [128, 3584, 1024], P('expert', None, 'tensor'), may hold values from -0.09375 to 0.09375
- w_out: bfloat16 [128, 1024, 3584], P('expert', 'tensor'), may hold values from -0.375 to 0.375
- routes: int32 [4096, 8], P('expert'), may hold values from 0 to 127, all different within a row; in each aligned block of 32 rows (0 to 31, 32 to 63, ...) at most 4 rows name the same one
- gate_weights: float32 [4096, 8], P('expert'), may hold values from 0.05 to 0.5
Outputs:
- layer_out: bfloat16 [4096, 3584], P('expert')
Inputs may be any that keep to these rules, and one draw needn't show every extreme that they name: `routes`: each row names 8 different experts. In each aligned block of 32 rows (the tokens of one index of expert) no expert is named by more than 4 rows, and in some block an expert is named by exactly 4 rows.
All inputs are finite; a program needn't handle non-finite values.
Results may differ from a plain program's by a relative error of at most 0.02.
Values may be sent and summed in bfloat16 or wider, within the bound.
No kernel may reach another device: no remote copies, remote signals or barrier semaphores. Data moves between devices by JAX's collectives and lax.ppermute only.
A program may use at most 64 MiB of HBM per device.

v0:
```python
import jax
import jax.numpy as jnp
from jax import lax
from jax.sharding import PartitionSpec as P

QB = 128
EPSILON = 1e-06


def capacity(group_tokens, top_count, expert_count):
    return min(group_tokens, max(4, 2 * group_tokens * top_count // expert_count))


def shards(attn_partial, residual_in, norm_gain, w_in, w_out, routes, gate_weights):
    group_tokens, top_count = routes.shape
    model_width = residual_in.shape[1]
    expert_count = lax.axis_size("expert")
    tensor_count = lax.axis_size("tensor")
    slot_count = capacity(group_tokens, top_count, expert_count)
    block_count = model_width // QB
    w_in_d = lax.all_to_all(w_in[0], "tensor", split_axis=0, concat_axis=1, tiled=True)
    w_out_d = lax.all_to_all(w_out[0], "tensor", split_axis=1, concat_axis=0, tiled=True)
    hidden_count = w_in_d.shape[1]
    hidden_quarter = hidden_count // tensor_count
    attention = lax.psum_scatter(
        attn_partial[0].astype(jnp.float32).astype(jnp.bfloat16),
        "tensor",
        scatter_dimension=0,
        tiled=True,
    ).astype(jnp.float32)
    residual = (residual_in.astype(jnp.float32) + attention).astype(jnp.bfloat16)
    stream = residual.astype(jnp.float32)
    rms_value = jnp.sqrt(jnp.mean(stream * stream, axis=1, keepdims=True) + EPSILON)
    normed = stream / rms_value * norm_gain.astype(jnp.float32)
    blocks = normed.reshape(-1, block_count, QB)
    block_scale = (jnp.max(jnp.abs(blocks), axis=2) + EPSILON).astype(jnp.bfloat16)
    scale_wide = block_scale.astype(jnp.float32)[:, :, None]
    quantized = (blocks / scale_wide).astype(jnp.bfloat16)
    expert_input = (
        (quantized.astype(jnp.float32) * scale_wide).reshape(-1, model_width).astype(jnp.bfloat16)
    )
    both = lax.all_to_all(
        jnp.stack([expert_input, residual]), "tensor", split_axis=2, concat_axis=1, tiled=True
    )
    group_input, group_resid = (both[0], both[1])
    pair_expert = routes.reshape(-1)
    onehot = (pair_expert[:, None] == jnp.arange(expert_count, dtype=jnp.int32)[None, :]).astype(
        jnp.int32
    )
    earlier = jnp.cumsum(onehot, axis=0) - onehot
    slot_index = jnp.sum(earlier * onehot, axis=1)
    target = pair_expert * slot_count + slot_index
    pair_total = group_tokens * top_count
    slot_table = (
        jnp.full((expert_count * slot_count,), -1, jnp.int32)
        .at[target]
        .set(jnp.arange(pair_total, dtype=jnp.int32))
    )
    slot_table = slot_table.reshape(expert_count, slot_count)
    filled = slot_table >= 0
    token_ids = jnp.maximum(slot_table, 0) // top_count
    row_block = jnp.where(filled[:, :, None], group_input[token_ids], jnp.zeros((), jnp.bfloat16))
    recv_rows = lax.all_to_all(row_block, "expert", split_axis=0, concat_axis=0, tiled=True)
    sources = recv_rows.shape[0]
    quarter = recv_rows.shape[2]
    rows = recv_rows.reshape(sources * slot_count, quarter)
    pre_partial = jnp.dot(rows, w_in_d, preferred_element_type=jnp.float32)
    pre_value = lax.psum_scatter(pre_partial, "tensor", scatter_dimension=1, tiled=True)
    hidden_part = jax.nn.silu(pre_value).astype(jnp.bfloat16)
    hidden = lax.all_gather(hidden_part, "tensor", axis=1, tiled=True)
    summed = jnp.zeros((rows.shape[0], quarter), jnp.float32)
    for lane in range(tensor_count):
        lo = lane * hidden_quarter
        term = jnp.dot(
            hidden[:, lo : lo + hidden_quarter],
            w_out_d[lo : lo + hidden_quarter],
            preferred_element_type=jnp.float32,
        ).astype(jnp.bfloat16)
        summed = summed + term.astype(jnp.float32)
    expert_out = summed.astype(jnp.bfloat16).reshape(sources, slot_count, quarter)
    returned = lax.all_to_all(expert_out, "expert", split_axis=0, concat_axis=0, tiled=True)
    flat_back = returned.reshape(expert_count * slot_count, quarter)
    picked = flat_back[target].astype(jnp.float32) * gate_weights.reshape(-1)[:, None]
    mixture = jnp.sum(picked.reshape(group_tokens, top_count, quarter), axis=1)
    out_part = (group_resid.astype(jnp.float32) + mixture).astype(jnp.bfloat16)
    return lax.all_gather(out_part, "tensor", axis=1, tiled=True)


def solution(mesh):
    return jax.shard_map(
        shards,
        mesh=mesh,
        in_specs=(
            P("tensor", "expert", None),
            P(("expert", "tensor"), None),
            P(),
            P("expert", None, "tensor"),
            P("expert", "tensor", None),
            P("expert", None),
            P("expert", None),
        ),
        out_specs=P("expert", None),
        check_vma=False,
    )
```

profile of v0, /device:TPU:10, one launch (start us, length us, event | category | flops | bytes accessed | tf_op | source)
XLA Modules:
  0.0 264.9 jit_solution(16002327998737600328)
XLA Ops:
  10.2 28.8 %reduce-scatter.3.cloned.1.call-done = bf16[8,3584]{1,0:T(8,128)(2,1)} async-done(((bf16[32,3584]{1,0:T(8,128)(2,1)}), bf16[8,3584]{1,0:T(8,128)(2,1)}) %reduce-scatter.3.cloned.1.call-update) | async-done | bytes 57360 | tf_op jit(solution)/shard_map/reduce_scatter | solution.py:25
  40.3 2.5 copy.44
  42.8 2.6 reshape.198
  45.4 5.7 %all-to-all-start = ((bf16[4,2,7168]{2,1,0:T(2,128)(2,1)}), bf16[4,2,7168]{2,1,0:T(2,128)(2,1)S(1)}, u32[]{:S(2)}, u32[]{:S(2)}) async-start(bf16[4,2,7168]{2,1,0:T(2,128)(2,1)} %reshape.198), calls=%async_computation.1 | async-start | bytes 229376 | tf_op jit(solution)/shard_map/all_to_all | solution.py:42
  51.3 4.3 %all-to-all-done = bf16[4,2,7168]{2,1,0:T(2,128)(2,1)S(1)} async-done(((bf16[4,2,7168]{2,1,0:T(2,128)(2,1)}), bf16[4,2,7168]{2,1,0:T(2,128)(2,1)S(1)}, u32[]{:S(2)}, u32[]{:S(2)}) %all-to-all-start) | async-done | bytes 114720 | tf_op jit(solution)/shard_map/all_to_all | solution.py:42
  55.6 5.0 %all-to-all-start.2 = ((bf16[4,896,256]{2,1,0:T(8,128)(2,1)}), bf16[4,896,256]{2,1,0:T(8,128)(2,1)S(1)}, u32[]{:S(2)}, u32[]{:S(2)}) async-start(bf16[4,896,256]{2,1,0:T(8,128)(2,1)} %bitcast.79), calls=%async_computation.3 | async-start | bytes 3670016 | tf_op jit(solution)/shard_map/all_to_all | solution.py:21
  62.5 3.4 %reshape.199 = bf16[3584,2,8]{2,1,0:T(2,128)(2,1)} reshape(bf16[4,2,7168]{2,1,0:T(2,128)(2,1)S(1)} %all-to-all-done) | data formatting | bytes 229376
  65.9 4.3 %copy.45 = bf16[2,8,4,896]{3,1,2,0:T(8,128)(2,1)S(1)} copy(bf16[2,8,4,896]{1,0,3,2:T(2,128)(2,1)} %bitcast.78) | data formatting | bytes 229376 | tf_op jit(solution)/shard_map/all_to_all | solution.py:42
  70.3 2.8 %gather_fusion = bf16[512,896]{1,0:T(8,128)(2,1)} fusion(bf16[32,896]{1,0:T(8,128)(2,1)S(1)} %slice_bitcast_fusion.8, s32[1024]{0:T(1024)S(1)} %pad_clamp_fusion.1), kind=kCustom, calls=%fused_computation | custom fusion | bytes 1837056 | tf_op jit(solution)/shard_map/gather | solution.py:62
  73.0 1.8 reshape.172
  76.3 3.2 %all-to-all-done.2 = bf16[4,896,256]{2,1,0:T(8,128)(2,1)S(1)} async-done(((bf16[4,896,256]{2,1,0:T(8,128)(2,1)}), bf16[4,896,256]{2,1,0:T(8,128)(2,1)S(1)}, u32[]{:S(2)}, u32[]{:S(2)}) %all-to-all-start.2) | async-done | bytes 1835040 | tf_op jit(solution)/shard_map/all_to_all | solution.py:21
  79.5 14.2 %all-to-all-start.1 = ((bf16[128,4,896]{2,1,0:T(4,128)(2,1)}), bf16[128,4,896]{2,1,0:T(4,128)(2,1)S(1)}, u32[]{:S(2)}, u32[]{:S(2)}) async-start(bf16[128,4,896]{2,1,0:T(4,128)(2,1)} %broadcast_select_fusion), calls=%async_computation.2 | async-start | bytes 1835008 | tf_op jit(solution)/shard_map/all_to_all | solution.py:63
  93.7 2.4 copy.51
  96.2 26.1 %all-to-all-done.1 = bf16[128,4,896]{2,1,0:T(4,128)(2,1)S(1)} async-done(((bf16[128,4,896]{2,1,0:T(4,128)(2,1)}), bf16[128,4,896]{2,1,0:T(4,128)(2,1)S(1)}, u32[]{:S(2)}, u32[]{:S(2)}) %all-to-all-start.1) | async-done | bytes 917536 | tf_op jit(solution)/shard_map/all_to_all | solution.py:63
  123.4 3.8 %fusion.20 = f32[512,1024]{1,0:T(8,128)} fusion(bf16[512,896]{1,0:T(8,128)(2,1)} %reshape.166, bf16[896,1024]{0,1:T(8,128)(2,1)S(1)} %bitcast.80), kind=kOutput, calls=%fused_computation.62 | convolution fusion | flops 939524096 | bytes 4849664 | tf_op jit(solution)/shard_map/dot_general | solution.py:67
  127.4 25.9 %reduce-scatter.5.cloned.1.call-done = f32[512,256]{1,0:T(8,128)} async-done(((f32[512,1024]{1,0:T(8,128)}), f32[512,256]{1,0:T(8,128)}) %reduce-scatter.5.cloned.1.call-update) | async-done | bytes 524304 | tf_op jit(solution)/shard_map/reduce_scatter | solution.py:68
  153.3 1.9 multiply_convert_fusion
  155.3 2.3 copy.52
  157.6 33.2 %all_to_all.60 = bf16[256,4,896]{0,2,1:T(8,128)(2,1)S(1)} all-to-all(bf16[256,4,896]{0,2,1:T(8,128)(2,1)} %bitcast.76), channel_id=1, replica_groups=mesh['expert'=128,'tensor'=4] {'tensor'}, dimensions={1} | all-to-all | bytes 3670016 | tf_op jit(solution)/shard_map/all_to_all | solution.py:22
  190.8 5.0 %all-gather.2.cloned.1.call-done = bf16[512,1024]{1,0:T(8,128)(2,1)} async-done(((bf16[512,256]{1,0:T(8,128)(2,1)}), bf16[512,1024]{1,0:T(8,128)(2,1)}) %all-gather.2.cloned.1.call-update) | async-done | bytes 1048592 | tf_op jit(solution)/shard_map/all_gather | solution.py:70
  195.8 1.5 convolution_convert_fusion.2
  201.0 14.2 %all-to-all-start.4 = ((bf16[128,4,896]{2,1,0:T(4,128)(2,1)}), bf16[128,4,896]{2,1,0:T(4,128)(2,1)S(1)}, u32[]{:S(2)}, u32[]{:S(2)}) async-start(bf16[128,4,896]{2,1,0:T(4,128)(2,1)} %reshape.167), calls=%async_computation.6 | async-start | bytes 1835008 | tf_op jit(solution)/shard_map/all_to_all | solution.py:81
  215.2 28.5 %all-to-all-done.4 = bf16[128,4,896]{2,1,0:T(4,128)(2,1)S(1)} async-done(((bf16[128,4,896]{2,1,0:T(4,128)(2,1)}), bf16[128,4,896]{2,1,0:T(4,128)(2,1)S(1)}, u32[]{:S(2)}, u32[]{:S(2)}) %all-to-all-start.4) | async-done | bytes 917536 | tf_op jit(solution)/shard_map/all_to_all | solution.py:81
  245.5 12.2 %all_gather.7 = bf16[32,3584]{1,0:T(8,128)(2,1)S(1)} all-gather(bf16[32,896]{1,0:T(8,128)(2,1)S(1)} %fusion.13), channel_id=1, replica_groups=mesh['expert'=128,'tensor'=4] {'tensor'}, dimensions={1}, use_global_device_ids=true | all-gather | bytes 286720 | tf_op jit(solution)/shard_map/all_gather | solution.py:86
  (61 shorter events, 16.1 us)
Async XLA Ops:
  6.5 32.4 %reduce-scatter.3.cloned.1.call-start = ((), (), s32[]{:S(2)}) async-start(), calls=%async_computation.7 | async-start | bytes 286720 | tf_op jit(solution)/shard_map/reduce_scatter | solution.py:25
  45.4 10.1 %all-to-all-start = ((bf16[4,2,7168]{2,1,0:T(2,128)(2,1)}), bf16[4,2,7168]{2,1,0:T(2,128)(2,1)S(1)}, u32[]{:S(2)}, u32[]{:S(2)}) async-start(bf16[4,2,7168]{2,1,0:T(2,128)(2,1)} %reshape.198), calls=%async_computation.1 | async-start | bytes 229376 | tf_op jit(solution)/shard_map/all_to_all | solution.py:42
  55.6 23.9 %all-to-all-start.2 = ((bf16[4,896,256]{2,1,0:T(8,128)(2,1)}), bf16[4,896,256]{2,1,0:T(8,128)(2,1)S(1)}, u32[]{:S(2)}, u32[]{:S(2)}) async-start(bf16[4,896,256]{2,1,0:T(8,128)(2,1)} %bitcast.79), calls=%async_computation.3 | async-start | bytes 3670016 | tf_op jit(solution)/shard_map/all_to_all | solution.py:21
  79.5 42.7 %all-to-all-start.1 = ((bf16[128,4,896]{2,1,0:T(4,128)(2,1)}), bf16[128,4,896]{2,1,0:T(4,128)(2,1)S(1)}, u32[]{:S(2)}, u32[]{:S(2)}) async-start(bf16[128,4,896]{2,1,0:T(4,128)(2,1)} %broadcast_select_fusion), calls=%async_computation.2 | async-start | bytes 1835008 | tf_op jit(solution)/shard_map/all_to_all | solution.py:63
  93.7 59.7 %reduce-scatter.5.cloned.1.call-start = ((), (), s32[]{:S(2)}) async-start(), calls=%async_computation.8 | async-start | bytes 2621440 | tf_op jit(solution)/shard_map/reduce_scatter | solution.py:68
  96.2 27.2 %copy-start.1 = (bf16[896,4,256]{0,2,1:T(8,128)(2,1)S(1)}, bf16[896,4,256]{0,2,1:T(8,128)(2,1)}, u32[]{:S(2)}) copy-start(bf16[896,4,256]{0,2,1:T(8,128)(2,1)} %copy.51) | copy-start | bytes 5505028
  127.2 28.1 %copy-start = (bf16[1,256,3584]{2,1,0:T(8,128)(2,1)S(1)}, bf16[1,256,3584]{2,1,0:T(8,128)(2,1)}, u32[]{:S(2)}) copy-start(bf16[1,256,3584]{2,1,0:T(8,128)(2,1)} %param.11) | copy-start | bytes 5505028
  127.2 68.6 %all-gather.2.cloned.1.call-start = ((), (), s32[]{:S(2)}) async-start(), calls=%async_computation.9 | async-start | bytes 1310720 | tf_op jit(solution)/shard_map/all_gather | solution.py:70
  195.8 2.9 %copy-start.2 = (bf16[512,1024]{1,0:T(8,128)(2,1)S(1)}, bf16[512,1024]{1,0:T(8,128)(2,1)}, u32[]{:S(2)}) copy-start(bf16[512,1024]{1,0:T(8,128)(2,1)} %all-gather.2.cloned.1.call-done) | copy-start | bytes 3145732
  199.8 15.3 %copy-start.3 = (f32[32,8]{0,1:T(8,128)S(1)}, f32[32,8]{0,1:T(8,128)}, u32[]{:S(2)}) copy-start(f32[32,8]{0,1:T(8,128)} %param.13) | copy-start | bytes 3076
  201.0 42.7 %all-to-all-start.4 = ((bf16[128,4,896]{2,1,0:T(4,128)(2,1)}), bf16[128,4,896]{2,1,0:T(4,128)(2,1)S(1)}, u32[]{:S(2)}, u32[]{:S(2)}) async-start(bf16[128,4,896]{2,1,0:T(4,128)(2,1)} %reshape.167), calls=%async_computation.6 | async-start | bytes 1835008 | tf_op jit(solution)/shard_map/all_to_all | solution.py:81
Sparse Core Ops, SparseCore 0:
  10.1 28.8 reduce-scatter.2
  127.3 25.9 reduce-scatter.4
  155.4 40.2 all-gather.1
where the time goes:
time: 266 us; the launch traced here: 265 us
  waiting for transfers between devices  122 us (46%)
  blocking collectives  45.5 us (17%)
  starting transfers between devices  39.3 us (15%)
  local copies, waits for them, and re-layouts  29.7 us (11%)
  between operations  13.4 us (5%)
  matrix products  7.82 us (3%)
  other arithmetic  6.91 us (3%)
    all_to_all x1, blocking collectives, shards(): lax.all_to_all(w_out[0], 'tensor', split_axis=1, concat_axis=0, tiled=True)  33.2 us
    reduce_scatter x1, waiting for transfers between devices, shards(): lax.psum_scatter(attn_partial[0].astype(jnp.float32).astype(jnp.bfloat16)...  28.8 us
    all_to_all x1, waiting for transfers between devices, shards(): lax.all_to_all(expert_out, 'expert', split_axis=0, concat_axis=0, tiled=T...  28.5 us
    all_to_all x1, waiting for transfers between devices, shards(): lax.all_to_all(row_block, 'expert', split_axis=0, concat_axis=0, tiled=True)  26.1 us
    reduce_scatter x1, waiting for transfers between devices, shards(): lax.psum_scatter(pre_partial, 'tensor', scatter_dimension=1, tiled=True)  25.9 us
    all_to_all x1, starting transfers between devices, shards(): lax.all_to_all(row_block, 'expert', split_axis=0, concat_axis=0, tiled=True)  14.2 us
    all_to_all x1, starting transfers between devices, shards(): lax.all_to_all(expert_out, 'expert', split_axis=0, concat_axis=0, tiled=T...  14.2 us
    all_gather x1, blocking collectives, shards(): return lax.all_gather(out_part, 'tensor', axis=1, tiled=True)  12.2 us
  transfers between devices with their start and end apart: 7, of which 7 were waited for; matrix products, arithmetic and copies ran while one was open for 9% of the time, Pallas kernels for 0%

commit v1 on v0

--- a/solution.py
+++ b/solution.py
@@ -1,3 +1,4 @@
+import functools
 import jax
 import jax.numpy as jnp
 from jax import lax
@@ -5,6 +6,34 @@
 
 QB = 128
 EPSILON = 1e-06
+
+
+def post_view(s0, ax_name):
+    devs = lax.axis_size(ax_name)
+    k0 = 0
+    table = []
+    while k0 < devs:
+        table.append((k0, (k0 + 1) % devs))
+        k0 += 1
+    grid = []
+    k0 = 0
+    while k0 < devs:
+        grid.append((k0, (k0 - 1) % devs))
+        k0 = k0 + 1
+    formed, part_now = ([s0], [s0])
+    for _ in range(devs // 2):
+        formed.append(lax.ppermute(formed[-1], ax_name, table))
+    rr = 0
+    while rr < (devs - 1) // 2:
+        part_now.append(lax.ppermute(part_now[-1], ax_name, grid))
+        rr = rr + 1
+    inter = jnp.concatenate([*formed[::-1], *part_now[1:]], axis=1)
+    a_now = lax.axis_index(ax_name)
+    carry = jnp.roll(inter, (a_now - devs // 2) * s0.shape[1], axis=1)
+    return carry
+
+
+register_the_masks = functools.partial(post_view, ax_name="tensor")
 
 
 def capacity(group_tokens, top_count, expert_count):
@@ -83,7 +112,7 @@
     picked = flat_back[target].astype(jnp.float32) * gate_weights.reshape(-1)[:, None]
     mixture = jnp.sum(picked.reshape(group_tokens, top_count, quarter), axis=1)
     out_part = (group_resid.astype(jnp.float32) + mixture).astype(jnp.bfloat16)
-    return lax.all_gather(out_part, "tensor", axis=1, tiled=True)
+    return register_the_masks(out_part)
 
 
 def solution(mesh):

time: 266 us -> 271 us (1.019)
  the two profiles are of different devices: /device:TPU:10 before, /device:TPU:14 now
where the time goes in v1:
time: 271 us; the launch traced here: 270 us
  waiting for transfers between devices  130 us (48%)
  starting transfers between devices  48 us (18%)
  blocking collectives  33.2 us (12%)
  local copies, waits for them, and re-layouts  29.9 us (11%)
  between operations  13.4 us (5%)
  matrix products  7.81 us (3%)
  other arithmetic  6.93 us (3%)
    all_to_all x1, blocking collectives, shards(): lax.all_to_all(w_out[0], 'tensor', split_axis=1, concat_axis=0, tiled=True)  33.2 us
    reduce_scatter x1, waiting for transfers between devices, shards(): lax.psum_scatter(attn_partial[0].astype(jnp.float32).astype(jnp.bfloat16)...  28.7 us
    all_to_all x1, waiting for transfers between devices, shards(): lax.all_to_all(expert_out, 'expert', split_axis=0, concat_axis=0, tiled=T...  28.5 us
    all_to_all x1, waiting for transfers between devices, shards(): lax.all_to_all(row_block, 'expert', split_axis=0, concat_axis=0, tiled=True)  26.1 us
    reduce_scatter x1, waiting for transfers between devices, shards(): lax.psum_scatter(pre_partial, 'tensor', scatter_dimension=1, tiled=True)  25.9 us
    all_to_all x1, starting transfers between devices, shards(): lax.all_to_all(expert_out, 'expert', split_axis=0, concat_axis=0, tiled=T...  14.2 us
    all_to_all x1, starting transfers between devices, shards(): lax.all_to_all(row_block, 'expert', split_axis=0, concat_axis=0, tiled=True)  14.2 us
    unnamed x21, local copies, waits for them, and re-layouts  9.27 us
  transfers between devices with their start and end apart: 10, of which 10 were waited for; matrix products, arithmetic and copies ran while one was open for 9% of the time, Pallas kernels for 0%

profile of v1, /device:TPU:14, one launch (start us, length us, event | category | flops | bytes accessed | tf_op | source)
XLA Modules:
  0.0 269.7 jit_solution(11239441242730784967)
XLA Ops:
  10.2 28.7 %reduce-scatter.3.cloned.1.call-done = bf16[8,3584]{1,0:T(8,128)(2,1)} async-done(((bf16[32,3584]{1,0:T(8,128)(2,1)}), bf16[8,3584]{1,0:T(8,128)(2,1)}) %reduce-scatter.3.cloned.1.call-update) | async-done | bytes 57360 | tf_op jit(solution)/shard_map/reduce_scatter | solution.py:54
  40.3 2.5 copy.44
  42.8 2.6 reshape.198
  45.4 5.7 %all-to-all-start = ((bf16[4,2,7168]{2,1,0:T(2,128)(2,1)}), bf16[4,2,7168]{2,1,0:T(2,128)(2,1)S(1)}, u32[]{:S(2)}, u32[]{:S(2)}) async-start(bf16[4,2,7168]{2,1,0:T(2,128)(2,1)} %reshape.198), calls=%async_computation.1 | async-start | bytes 229376 | tf_op jit(solution)/shard_map/all_to_all | solution.py:71
  51.3 3.6 %all-to-all-done = bf16[4,2,7168]{2,1,0:T(2,128)(2,1)S(1)} async-done(((bf16[4,2,7168]{2,1,0:T(2,128)(2,1)}), bf16[4,2,7168]{2,1,0:T(2,128)(2,1)S(1)}, u32[]{:S(2)}, u32[]{:S(2)}) %all-to-all-start) | async-done | bytes 114720 | tf_op jit(solution)/shard_map/all_to_all | solution.py:71
  54.9 5.6 %all-to-all-start.2 = ((bf16[4,896,256]{2,1,0:T(8,128)(2,1)}), bf16[4,896,256]{2,1,0:T(8,128)(2,1)S(1)}, u32[]{:S(2)}, u32[]{:S(2)}) async-start(bf16[4,896,256]{2,1,0:T(8,128)(2,1)} %bitcast.79), calls=%async_computation.3 | async-start | bytes 3670016 | tf_op jit(solution)/shard_map/all_to_all | solution.py:50
  62.5 3.4 %reshape.199 = bf16[3584,2,8]{2,1,0:T(2,128)(2,1)} reshape(bf16[4,2,7168]{2,1,0:T(2,128)(2,1)S(1)} %all-to-all-done) | data formatting | bytes 229376
  65.9 4.3 %copy.45 = bf16[2,8,4,896]{3,1,2,0:T(8,128)(2,1)S(1)} copy(bf16[2,8,4,896]{1,0,3,2:T(2,128)(2,1)} %bitcast.78) | data formatting | bytes 229376 | tf_op jit(solution)/shard_map/all_to_all | solution.py:71
  70.2 2.8 %gather_fusion = bf16[512,896]{1,0:T(8,128)(2,1)} fusion(bf16[32,896]{1,0:T(8,128)(2,1)S(1)} %slice_bitcast_fusion.8, s32[1024]{0:T(1024)S(1)} %pad_clamp_fusion.1), kind=kCustom, calls=%fused_computation | custom fusion | bytes 1837056 | tf_op jit(solution)/shard_map/gather | solution.py:91
  76.3 2.6 all-to-all-done.2
  78.8 14.2 %all-to-all-start.1 = ((bf16[128,4,896]{2,1,0:T(4,128)(2,1)}), bf16[128,4,896]{2,1,0:T(4,128)(2,1)S(1)}, u32[]{:S(2)}, u32[]{:S(2)}) async-start(bf16[128,4,896]{2,1,0:T(4,128)(2,1)} %broadcast_select_fusion), calls=%async_computation.2 | async-start | bytes 1835008 | tf_op jit(solution)/shard_map/all_to_all | solution.py:92
  93.0 2.4 copy.51
  95.5 26.1 %all-to-all-done.1 = bf16[128,4,896]{2,1,0:T(4,128)(2,1)S(1)} async-done(((bf16[128,4,896]{2,1,0:T(4,128)(2,1)}), bf16[128,4,896]{2,1,0:T(4,128)(2,1)S(1)}, u32[]{:S(2)}, u32[]{:S(2)}) %all-to-all-start.1) | async-done | bytes 917536 | tf_op jit(solution)/shard_map/all_to_all | solution.py:92
  122.7 3.8 %fusion.20 = f32[512,1024]{1,0:T(8,128)} fusion(bf16[512,896]{1,0:T(8,128)(2,1)} %reshape.166, bf16[896,1024]{0,1:T(8,128)(2,1)S(1)} %bitcast.80), kind=kOutput, calls=%fused_computation.71 | convolution fusion | flops 939524096 | bytes 4849664 | tf_op jit(solution)/shard_map/dot_general | solution.py:96
  126.8 25.9 %reduce-scatter.5.cloned.1.call-done = f32[512,256]{1,0:T(8,128)} async-done(((f32[512,1024]{1,0:T(8,128)}), f32[512,256]{1,0:T(8,128)}) %reduce-scatter.5.cloned.1.call-update) | async-done | bytes 524304 | tf_op jit(solution)/shard_map/reduce_scatter | solution.py:97
  154.6 2.3 copy.52
  156.9 33.2 %all_to_all.60 = bf16[256,4,896]{0,2,1:T(8,128)(2,1)S(1)} all-to-all(bf16[256,4,896]{0,2,1:T(8,128)(2,1)} %bitcast.76), channel_id=1, replica_groups=mesh['expert'=128,'tensor'=4] {'tensor'}, dimensions={1} | all-to-all | bytes 3670016 | tf_op jit(solution)/shard_map/all_to_all | solution.py:51
  190.2 5.5 %all-gather.2.cloned.1.call-done = bf16[512,1024]{1,0:T(8,128)(2,1)} async-done(((bf16[512,256]{1,0:T(8,128)(2,1)}), bf16[512,1024]{1,0:T(8,128)(2,1)}) %all-gather.2.cloned.1.call-update) | async-done | bytes 1048592 | tf_op jit(solution)/shard_map/all_gather | solution.py:99
  200.9 14.2 %all-to-all-start.4 = ((bf16[128,4,896]{2,1,0:T(4,128)(2,1)}), bf16[128,4,896]{2,1,0:T(4,128)(2,1)S(1)}, u32[]{:S(2)}, u32[]{:S(2)}) async-start(bf16[128,4,896]{2,1,0:T(4,128)(2,1)} %reshape.167), calls=%async_computation.6 | async-start | bytes 1835008 | tf_op jit(solution)/shard_map/all_to_all | solution.py:110
  215.2 28.5 %all-to-all-done.4 = bf16[128,4,896]{2,1,0:T(4,128)(2,1)S(1)} async-done(((bf16[128,4,896]{2,1,0:T(4,128)(2,1)}), bf16[128,4,896]{2,1,0:T(4,128)(2,1)S(1)}, u32[]{:S(2)}, u32[]{:S(2)}) %all-to-all-start.4) | async-done | bytes 917536 | tf_op jit(solution)/shard_map/all_to_all | solution.py:110
  247.6 3.8 %collective-permute-done = bf16[32,896]{1,0:T(8,128)(2,1)S(1)} collective-permute-done((bf16[32,896]{1,0:T(8,128)(2,1)S(1)}, bf16[32,896]{1,0:T(8,128)(2,1)S(1)}, u32[]{:S(2)}, u32[]{:S(2)}) %collective-permute-start) | collective-permute-done | bytes 57376 | tf_op jit(solution)/shard_map/ppermute | solution.py:25
  251.5 3.4 %collective-permute-start.1 = (bf16[32,896]{1,0:T(8,128)(2,1)S(1)}, bf16[32,896]{1,0:T(8,128)(2,1)S(1)}, u32[]{:S(2)}, u32[]{:S(2)}) collective-permute-start(bf16[32,896]{1,0:T(8,128)(2,1)S(1)} %collective-permute-done), channel_id=1, source_target_pairs={{0,1},{1,2},{2,3},{3,0},{4,5},{5,6},{6,7},{7,4},{8,9},{9,10},{10,1... | collective-permute-start | bytes 172040 | tf_op jit(solution)/shard_map/ppermute | solution.py:25
  254.9 2.4 collective-permute-start.2
  257.6 4.6 %collective-permute-done.2 = bf16[32,896]{1,0:T(8,128)(2,1)S(1)} collective-permute-done((bf16[32,896]{1,0:T(8,128)(2,1)S(1)}, bf16[32,896]{1,0:T(8,128)(2,1)S(1)}, u32[]{:S(2)}, u32[]{:S(2)}) %collective-permute-start.2) | collective-permute-done | bytes 57376 | tf_op jit(solution)/shard_map/ppermute | solution.py:28
  (74 shorter events, 23.9 us)
Async XLA Ops:
  6.5 32.4 %reduce-scatter.3.cloned.1.call-start = ((), (), s32[]{:S(2)}) async-start(), calls=%async_computation.7 | async-start | bytes 286720 | tf_op jit(solution)/shard_map/reduce_scatter | solution.py:54
  45.4 9.5 %all-to-all-start = ((bf16[4,2,7168]{2,1,0:T(2,128)(2,1)}), bf16[4,2,7168]{2,1,0:T(2,128)(2,1)S(1)}, u32[]{:S(2)}, u32[]{:S(2)}) async-start(bf16[4,2,7168]{2,1,0:T(2,128)(2,1)} %reshape.198), calls=%async_computation.1 | async-start | bytes 229376 | tf_op jit(solution)/shard_map/all_to_all | solution.py:71
  54.9 23.9 %all-to-all-start.2 = ((bf16[4,896,256]{2,1,0:T(8,128)(2,1)}), bf16[4,896,256]{2,1,0:T(8,128)(2,1)S(1)}, u32[]{:S(2)}, u32[]{:S(2)}) async-start(bf16[4,896,256]{2,1,0:T(8,128)(2,1)} %bitcast.79), calls=%async_computation.3 | async-start | bytes 3670016 | tf_op jit(solution)/shard_map/all_to_all | solution.py:50
  78.8 42.7 %all-to-all-start.1 = ((bf16[128,4,896]{2,1,0:T(4,128)(2,1)}), bf16[128,4,896]{2,1,0:T(4,128)(2,1)S(1)}, u32[]{:S(2)}, u32[]{:S(2)}) async-start(bf16[128,4,896]{2,1,0:T(4,128)(2,1)} %broadcast_select_fusion), calls=%async_computation.2 | async-start | bytes 1835008 | tf_op jit(solution)/shard_map/all_to_all | solution.py:92
  93.0 59.7 %reduce-scatter.5.cloned.1.call-start = ((), (), s32[]{:S(2)}) async-start(), calls=%async_computation.8 | async-start | bytes 2621440 | tf_op jit(solution)/shard_map/reduce_scatter | solution.py:97
  95.5 27.2 %copy-start.1 = (bf16[896,4,256]{0,2,1:T(8,128)(2,1)S(1)}, bf16[896,4,256]{0,2,1:T(8,128)(2,1)}, u32[]{:S(2)}) copy-start(bf16[896,4,256]{0,2,1:T(8,128)(2,1)} %copy.51) | copy-start | bytes 5505028
  126.5 28.1 %copy-start = (bf16[1,256,3584]{2,1,0:T(8,128)(2,1)S(1)}, bf16[1,256,3584]{2,1,0:T(8,128)(2,1)}, u32[]{:S(2)}) copy-start(bf16[1,256,3584]{2,1,0:T(8,128)(2,1)} %param.11) | copy-start | bytes 5505028
  126.5 69.2 %all-gather.2.cloned.1.call-start = ((), (), s32[]{:S(2)}) async-start(), calls=%async_computation.9 | async-start | bytes 1310720 | tf_op jit(solution)/shard_map/all_gather | solution.py:99
  195.7 2.9 %copy-start.2 = (bf16[512,1024]{1,0:T(8,128)(2,1)S(1)}, bf16[512,1024]{1,0:T(8,128)(2,1)}, u32[]{:S(2)}) copy-start(bf16[512,1024]{1,0:T(8,128)(2,1)} %all-gather.2.cloned.1.call-done) | copy-start | bytes 3145732
  199.7 15.3 %copy-start.3 = (f32[32,8]{0,1:T(8,128)S(1)}, f32[32,8]{0,1:T(8,128)}, u32[]{:S(2)}) copy-start(f32[32,8]{0,1:T(8,128)} %param.13) | copy-start | bytes 3076
  200.9 42.7 %all-to-all-start.4 = ((bf16[128,4,896]{2,1,0:T(4,128)(2,1)}), bf16[128,4,896]{2,1,0:T(4,128)(2,1)S(1)}, u32[]{:S(2)}, u32[]{:S(2)}) async-start(bf16[128,4,896]{2,1,0:T(4,128)(2,1)} %reshape.167), calls=%async_computation.6 | async-start | bytes 1835008 | tf_op jit(solution)/shard_map/all_to_all | solution.py:110
  245.4 6.1 %collective-permute-start = (bf16[32,896]{1,0:T(8,128)(2,1)S(1)}, bf16[32,896]{1,0:T(8,128)(2,1)S(1)}, u32[]{:S(2)}, u32[]{:S(2)}) collective-permute-start(bf16[32,896]{1,0:T(8,128)(2,1)S(1)} %fusion.13), channel_id=1, source_target_pairs={{0,1},{1,2},{2,3},{3,0},{4,5},{5,6},{6,7},{7,4},{8,9},{9,10},{10,1... | collective-permute-start | bytes 172040 | tf_op jit(solution)/shard_map/ppermute | solution.py:25
  251.5 6.1 %collective-permute-start.1 = (bf16[32,896]{1,0:T(8,128)(2,1)S(1)}, bf16[32,896]{1,0:T(8,128)(2,1)S(1)}, u32[]{:S(2)}, u32[]{:S(2)}) collective-permute-start(bf16[32,896]{1,0:T(8,128)(2,1)S(1)} %collective-permute-done), channel_id=1, source_target_pairs={{0,1},{1,2},{2,3},{3,0},{4,5},{5,6},{6,7},{7,4},{8,9},{9,10},{10,1... | collective-permute-start | bytes 172040 | tf_op jit(solution)/shard_map/ppermute | solution.py:25
  254.9 7.3 %collective-permute-start.2 = (bf16[32,896]{1,0:T(8,128)(2,1)S(1)}, bf16[32,896]{1,0:T(8,128)(2,1)S(1)}, u32[]{:S(2)}, u32[]{:S(2)}) collective-permute-start(bf16[32,896]{1,0:T(8,128)(2,1)S(1)} %fusion.13), channel_id=1, source_target_pairs={{0,3},{1,0},{2,1},{3,2},{4,7},{5,4},{6,5},{7,6},{8,11},{9,8},{10,9... | collective-permute-start | bytes 172040 | tf_op jit(solution)/shard_map/ppermute | solution.py:28
Sparse Core Ops, SparseCore 0:
  10.1 28.7 reduce-scatter.2
  126.7 25.9 reduce-scatter.4
  154.8 40.8 all-gather.1
